TPU v7x, 32 devices: a whole 2x2x4 slice. The times are simulated.
32 devices in a mesh: grp: 2 (over y), blk: 8 (over z, x), bin: 2 (over core).
Axes of the slice: x: 2, y: 2, z: 4, core: 2. Of those that a mesh axis runs over, the one named last changes fastest.
Arguments:
- units: bfloat16 [1024, 32768], P(('grp', 'bin'), 'blk'), parts along dimension 0, may hold values from -6 to 6
- cotangent: bfloat16 [1024, 32768], P(('grp', 'bin'), 'blk'), parts along dimension 0, may hold values from -6 to 6
- left_factor: bfloat16 [64, 512, 512], P('blk', 'bin'), may hold values from -0.25 to 0.25
- right_factor: bfloat16 [512, 64, 64], P('blk', 'bin'), may hold values from -0.75 to 0.75
- session_units: int32 [128], P(('grp', 'blk')), parts along dimension 0, may hold values from 128 to 512, as said below
Outputs:
- grad_left: bfloat16 [128, 512, 512], P(('grp', 'blk'), 'bin'), parts along dimension 0
- grad_right: bfloat16 [1024, 64, 64], P(('grp', 'blk'), 'bin'), parts along dimension 0
There are 2 independent parts, one for each index of `grp`. A program takes and returns all parts, laid end to end along the dimension named above; an argument that names none is the same for every part. Nothing has to cross between parts.
Inputs may be any that keep to these rules, and one draw needn't show every extreme that they name: `session_units`: each count is a multiple of a quarter of 512; some session of every group has all 512 units live.
All inputs are finite; a program needn't handle non-finite values.
Results may differ from a plain program's by a relative error of at most 0.0049.
Values may be sent and summed in bfloat16 or wider, within the bound.
No kernel may reach another device: no remote copies, remote signals or barrier semaphores. Data moves between devices by JAX's collectives and lax.ppermute only.
A program may use at most 128 MiB of HBM per device.

v0:
```python
import jax
import jax.numpy as jnp
from jax import lax
from jax.sharding import PartitionSpec as P


def on_device(units, cotangent, left_factor, right_factor, session_units):
    row_count = units.shape[0]
    local_blocks = left_factor.shape[0]
    block_size = left_factor.shape[2]
    right_local = right_factor.shape[0]
    order_right = right_factor.shape[2]
    peer_count = lax.axis_size("blk")
    unit_mask = (jnp.arange(block_size)[None, :] < session_units[:, None]).astype(jnp.bfloat16)
    inputs = units.reshape(row_count, local_blocks, block_size) * unit_mask[None]
    left_full = lax.all_gather(left_factor, "bin", axis=1, tiled=True)
    mixed = jnp.einsum(
        "rki,kij->kjr", inputs, left_full, preferred_element_type=jnp.float32
    ).astype(jnp.bfloat16)
    mixed_sent = mixed.reshape(local_blocks, peer_count, right_local, row_count)
    mixed_got = lax.all_to_all(mixed_sent, "blk", split_axis=1, concat_axis=0, tiled=True)
    permuted = mixed_got.reshape(order_right, right_local, row_count)
    upstream = cotangent.reshape(row_count, right_local, order_right)
    right_full = lax.all_gather(right_factor, "bin", axis=1, tiled=True)
    back_grad = jnp.einsum(
        "rjm,jkm->jkr", upstream, right_full, preferred_element_type=jnp.float32
    ).astype(jnp.bfloat16)
    back_sent = back_grad.reshape(right_local, peer_count, local_blocks, row_count)
    back_got = lax.all_to_all(back_sent, "blk", split_axis=1, concat_axis=0, tiled=True)
    returned = back_got.reshape(block_size, local_blocks, row_count)
    right_term = jnp.einsum("kjr,rjm->jkm", permuted, upstream, preferred_element_type=jnp.float32)
    grad_right = lax.psum_scatter(right_term, "bin", scatter_dimension=1, tiled=True).astype(
        jnp.bfloat16
    )
    left_term = jnp.einsum("rki,jkr->kij", inputs, returned, preferred_element_type=jnp.float32)
    grad_left = lax.psum_scatter(left_term, "bin", scatter_dimension=1, tiled=True).astype(
        jnp.bfloat16
    )
    return (grad_left, grad_right)


def solution(mesh):
    placed = (
        P(("grp", "bin"), "blk"),
        P(("grp", "bin"), "blk"),
        P("blk", "bin", None),
        P("blk", "bin", None),
        P(("grp", "blk")),
    )
    return jax.shard_map(
        on_device,
        mesh=mesh,
        in_specs=placed,
        out_specs=(P(("grp", "blk"), "bin", None), P(("grp", "blk"), "bin", None)),
        check_vma=False,
    )
```

profile of v0, /device:TPU:0, one launch (start us, length us, event | category | flops | bytes accessed | tf_op | source)
XLA Modules:
  0.0 175.1 jit_solution(1585854343197089779)
XLA Ops:
  7.2 0.0 copy-start.3
  7.2 0.0 copy-start
  7.2 0.0 all-gather.2.cloned.1.call-start
  7.2 0.7 all-gather.2.cloned.1.call-update
  7.9 0.0 copy-done.3
  7.9 0.1 fusion.6
  8.0 18.0 %all-gather.2.cloned.1.call-done = bf16[8,512,512]{2,1,0:T(8,128)(2,1)} async-done(((bf16[8,256,512]{2,1,0:T(8,128)(2,1)}), bf16[8,512,512]{2,1,0:T(8,128)(2,1)}) %all-gather.2.cloned.1.call-update) | async-done | bytes 4194320 | tf_op jit(solution)/shard_map/all_gather | solution.py:16
  26.0 0.0 copy-done
  26.0 4.8 %convert_bitcast_fusion = bf16[8,512,256]{1,2,0:T(8,128)(2,1)} fusion(bf16[8,512,512]{2,1,0:T(8,128)(2,1)} %all-gather.2.cloned.1.call-done, bf16[32,8,8,512]{3,2,1,0:T(8,128)(2,1)S(1)} %bitcast.30, bf16[8,512]{1,0:T(8,128)(2,1)S(1)} %fusion.6), kind=kOutput, calls=%fused_computation.4 | convolution fusion | flops 1075838976 | bytes 8396800 | tf_op jit(solution)/shard_map/rki,kij->kjr/dot_general | solution.py:17
  30.7 2.8 %copy.24 = bf16[8,512,256]{2,1,0:T(8,128)(2,1)S(1)} copy(bf16[8,512,256]{1,2,0:T(8,128)(2,1)} %convert_bitcast_fusion) | data formatting | bytes 4194304 | tf_op jit(solution)/shard_map/convert_element_type | solution.py:19
  33.6 1.5 copy.25
  35.1 5.8 %all-to-all-start.1 = ((bf16[8,8,64,256]{3,2,0,1:T(8,128)(2,1)}), bf16[8,8,64,256]{3,2,0,1:T(8,128)(2,1)}, u32[]{:S(2)}, u32[]{:S(2)}) async-start(bf16[8,8,64,256]{3,2,0,1:T(8,128)(2,1)} %copy.25), calls=%async_computation.2 | async-start | bytes 4194304 | tf_op jit(solution)/shard_map/all_to_all | solution.py:21
  40.8 0.0 copy-start.2
  40.8 3.3 %copy.20 = bf16[256,4096]{0,1:T(8,128)(2,1)S(1)} copy(bf16[256,4096]{1,0:T(8,128)(2,1)} %param.6) | data formatting | bytes 4194304 | tf_op args[1]
  44.2 0.0 copy-done.2
  44.2 2.6 %all_gather.6 = bf16[64,64,64]{2,1,0:T(8,128)(2,1)S(1)} all-gather(bf16[64,32,64]{2,1,0:T(8,128)(2,1)S(1)} %copy-done.2), channel_id=1, replica_groups=mesh['grp'=2,'blk'=8,'bin'=2] {'bin'}, dimensions={1}, use_global_device_ids=true | all-gather | bytes 786432 | tf_op jit(solution)/shard_map/all_gather | solution.py:24
  46.7 0.7 convert_bitcast_fusion.1
  47.4 1.5 copy.21
  48.9 40.7 %all-to-all-done.1 = bf16[8,8,64,256]{3,2,0,1:T(8,128)(2,1)} async-done(((bf16[8,8,64,256]{3,2,0,1:T(8,128)(2,1)}), bf16[8,8,64,256]{3,2,0,1:T(8,128)(2,1)}, u32[]{:S(2)}, u32[]{:S(2)}) %all-to-all-start.1) | async-done | bytes 2097184 | tf_op jit(solution)/shard_map/all_to_all | solution.py:21
  89.6 4.4 %all-to-all-start = ((bf16[64,8,8,256]{3,2,0,1:T(8,128)(2,1)}), bf16[64,8,8,256]{3,2,0,1:T(8,128)(2,1)}, u32[]{:S(2)}, u32[]{:S(2)}) async-start(bf16[64,8,8,256]{3,2,0,1:T(8,128)(2,1)} %copy.21), calls=%async_computation | async-start | bytes 4194304 | tf_op jit(solution)/shard_map/all_to_all | solution.py:29
  94.0 0.0 reduce-scatter.5.cloned.1.call-start
  94.0 4.3 %fusion = f32[64,64,64]{2,1,0:T(8,128)} fusion(bf16[256,64,64]{0,2,1:T(8,128)(2,1)S(1)} %bitcast.27, bf16[8,8,1,64,256]{4,3,1,0,2:T(8,128)(2,1)} %bitcast.8), kind=kOutput, calls=%fused_computation.1 | convolution fusion | flops 134217728 | bytes 5242880 | tf_op jit(solution)/shard_map/kjr,rjm->jkm/dot_general | solution.py:31
  98.3 0.0 reduce-scatter.5.cloned.1.call-update
  98.4 0.0 reduce-scatter.3.cloned.1.call-start
  98.4 43.4 %all-to-all-done = bf16[64,8,8,256]{3,2,0,1:T(8,128)(2,1)} async-done(((bf16[64,8,8,256]{3,2,0,1:T(8,128)(2,1)}), bf16[64,8,8,256]{3,2,0,1:T(8,128)(2,1)}, u32[]{:S(2)}, u32[]{:S(2)}) %all-to-all-start) | async-done | bytes 2097184 | tf_op jit(solution)/shard_map/all_to_all | solution.py:29
  141.8 0.0 copy-start.1
  141.8 2.2 %copy.22 = bf16[8,64,1,8,256]{4,1,0,3,2:T(8,128)(2,1)S(1)} copy(bf16[8,64,1,8,256]{4,3,1,0,2:T(8,128)(2,1)} %bitcast.3) | data formatting | bytes 4194304 | tf_op jit(solution)/shard_map/all_to_all | solution.py:29
  144.1 0.0 copy-done.1
  144.1 4.7 %fusion.3 = f32[8,512,512]{2,1,0:T(8,128)} fusion(bf16[512,8,256]{2,0,1:T(8,128)(2,1)S(1)} %bitcast.29, bf16[32,8,8,512]{3,2,1,0:T(8,128)(2,1)S(1)} %bitcast.31, bf16[8,512]{1,0:T(8,128)(2,1)S(1)} %fusion.6), kind=kOutput, calls=%fused_computation.6 | convolution fusion | flops 1074790400 | bytes 12591104 | tf_op jit(solution)/shard_map/rki,jkr->kij/dot_general | solution.py:35
  148.8 0.0 reduce-scatter.3.cloned.1.call-update
  148.8 0.0 reduce-scatter.5.cloned.1.call-done
  148.8 2.1 %convert_element_type.27 = bf16[64,32,64]{2,1,0:T(8,128)(2,1)} convert(f32[64,32,64]{2,1,0:T(8,128)} %reduce-scatter.5.cloned.1.call-done) | non-fusion elementwise | flops 131072 | bytes 786432 | tf_op jit(solution)/shard_map/convert_element_type | solution.py:32
  150.9 13.8 %reduce-scatter.3.cloned.1.call-done = f32[8,256,512]{2,1,0:T(8,128)} async-done(((f32[8,512,512]{2,1,0:T(8,128)}), f32[8,256,512]{2,1,0:T(8,128)}) %reduce-scatter.3.cloned.1.call-update) | async-done | bytes 4194320 | tf_op jit(solution)/shard_map/reduce_scatter | solution.py:36
  164.8 3.8 %convert_element_type.24 = bf16[8,256,512]{2,1,0:T(8,128)(2,1)} convert(f32[8,256,512]{2,1,0:T(8,128)} %reduce-scatter.3.cloned.1.call-done) | non-fusion elementwise | flops 1048576 | bytes 6291456 | tf_op jit(solution)/shard_map/convert_element_type | solution.py:36
Async XLA Ops:
  7.2 0.8 copy-start.3
  7.2 18.8 %copy-start = (bf16[256,4096]{1,0:T(8,128)(2,1)S(1)}, bf16[256,4096]{1,0:T(8,128)(2,1)}, u32[]{:S(2)}) copy-start(bf16[256,4096]{1,0:T(8,128)(2,1)} %param.5) | copy-start | bytes 6291460
  7.2 18.8 %all-gather.2.cloned.1.call-start = ((), (), s32[]{:S(2)}) async-start(), calls=%async_computation.5 | async-start | bytes 6291456 | tf_op jit(solution)/shard_map/all_gather | solution.py:16
  35.1 54.6 %all-to-all-start.1 = ((bf16[8,8,64,256]{3,2,0,1:T(8,128)(2,1)}), bf16[8,8,64,256]{3,2,0,1:T(8,128)(2,1)}, u32[]{:S(2)}, u32[]{:S(2)}) async-start(bf16[8,8,64,256]{3,2,0,1:T(8,128)(2,1)} %copy.25), calls=%async_computation.2 | async-start | bytes 4194304 | tf_op jit(solution)/shard_map/all_to_all | solution.py:21
  40.8 3.3 %copy-start.2 = (bf16[64,32,64]{2,1,0:T(8,128)(2,1)S(1)}, bf16[64,32,64]{2,1,0:T(8,128)(2,1)}, u32[]{:S(2)}) copy-start(bf16[64,32,64]{2,1,0:T(8,128)(2,1)} %param.8) | copy-start | bytes 786436
  89.6 52.2 %all-to-all-start = ((bf16[64,8,8,256]{3,2,0,1:T(8,128)(2,1)}), bf16[64,8,8,256]{3,2,0,1:T(8,128)(2,1)}, u32[]{:S(2)}, u32[]{:S(2)}) async-start(bf16[64,8,8,256]{3,2,0,1:T(8,128)(2,1)} %copy.21), calls=%async_computation | async-start | bytes 4194304 | tf_op jit(solution)/shard_map/all_to_all | solution.py:29
  94.0 54.8 %reduce-scatter.5.cloned.1.call-start = ((), (), s32[]{:S(2)}) async-start(), calls=%async_computation.6 | async-start | bytes 3145728 | tf_op jit(solution)/shard_map/reduce_scatter | solution.py:32
  98.4 66.4 %reduce-scatter.3.cloned.1.call-start = ((), (), s32[]{:S(2)}) async-start(), calls=%async_computation.4 | async-start | bytes 12582912 | tf_op jit(solution)/shard_map/reduce_scatter | solution.py:36
  141.8 2.2 %copy-start.1 = (bf16[256,4096]{1,0:T(8,128)(2,1)S(1)}, bf16[256,4096]{1,0:T(8,128)(2,1)}, u32[]{:S(2)}) copy-start(bf16[256,4096]{1,0:T(8,128)(2,1)} %param.5) | copy-start | bytes 6291460
Sparse Core Ops, SparseCore 0:
  9.6 16.3 all-gather.1
  98.5 10.8 reduce-scatter.4
  148.9 15.8 reduce-scatter.2
where the time goes:
time: 176 us; the launch traced here: 175 us
  waiting for transfers between devices  117 us (66%)
  matrix products  14.4 us (8%)
  between operations  13.8 us (8%)
  local copies, waits for them, and re-layouts  11.3 us (6%)
  starting transfers between devices  10.2 us (6%)
  other arithmetic  5.95 us (3%)
  blocking collectives  2.56 us (1%)
    all_to_all x1, waiting for transfers between devices, on_device(): lax.all_to_all(back_sent, 'blk', split_axis=1, concat_axis=0, tiled=True)  43.4 us
    all_to_all x1, waiting for transfers between devices, on_device(): lax.all_to_all(mixed_sent, 'blk', split_axis=1, concat_axis=0, tiled=True)  40.7 us
    all_gather x1, waiting for transfers between devices, on_device(): left_full = lax.all_gather(left_factor, 'bin', axis=1, tiled=True)  18 us
    reduce_scatter x1, waiting for transfers between devices, on_device(): lax.psum_scatter(left_term, 'bin', scatter_dimension=1, tiled=True)  13.8 us
    all_to_all x1, starting transfers between devices, on_device(): lax.all_to_all(mixed_sent, 'blk', split_axis=1, concat_axis=0, tiled=True)  5.77 us
    dot_general x1, matrix products, on_device(): jnp.einsum('rki,kij->kjr', inputs, left_full, preferred_element_type=jnp....  4.76 us
    dot_general x1, matrix products, on_device(): jnp.einsum('rki,jkr->kij', inputs, returned, preferred_element_type=jnp.f...  4.66 us
    all_to_all x1, starting transfers between devices, on_device(): lax.all_to_all(back_sent, 'blk', split_axis=1, concat_axis=0, tiled=True)  4.36 us
  transfers between devices with their start and end apart: 5, of which 4 were waited for; matrix products, arithmetic and copies ran while one was open for 11% of the time, Pallas kernels for 0%

commit v1 on v0

--- a/solution.py
+++ b/solution.py
@@ -1,7 +1,44 @@
+import functools
 import jax
 import jax.numpy as jnp
 from jax import lax
 from jax.sharding import PartitionSpec as P
+from jax.lax import axis_index, axis_size, ppermute
+
+
+def update_turns(inp, along_dim, shard_in):
+    current_value, before = (inp.shape[:along_dim], inp.shape[along_dim + 1 :])
+    aux = jnp.moveaxis(inp.reshape(*current_value, shard_in, -1, *before), along_dim, 0)
+    return aux
+
+
+def list_squares(view, ndim_at):
+    view = jnp.moveaxis(view, 0, ndim_at)
+    small = view.shape
+    local_next = view.reshape(
+        *small[:ndim_at], small[ndim_at] * small[ndim_at + 1], *small[ndim_at + 2 :]
+    )
+    return local_next
+
+
+def step_on_series_all(slab_in, axis_id, panel, target):
+    side_arr, k_now = (axis_size(axis_id), axis_index(axis_id))
+    u_next = update_turns(slab_in, panel, side_arr)
+    all_rows = u_next
+    for k in range(1, side_arr):
+        t1, v_next = ((k_now + k) % side_arr, (k_now - k) % side_arr)
+        top = lax.dynamic_index_in_dim(u_next, t1, 0)
+        arr_out = ppermute(
+            top,
+            axis_name=axis_id,
+            perm=list(map(lambda pp: (pp, (pp + k) % side_arr), range(side_arr))),
+        )
+        all_rows = lax.dynamic_update_slice_in_dim(all_rows, arr_out, v_next, axis=0)
+    q_next = list_squares(all_rows, target)
+    return q_next
+
+
+perform_layers_all = functools.partial(step_on_series_all, axis_id="blk", panel=1, target=0)
 
 
 def on_device(units, cotangent, left_factor, right_factor, session_units):
@@ -18,7 +55,7 @@
         "rki,kij->kjr", inputs, left_full, preferred_element_type=jnp.float32
     ).astype(jnp.bfloat16)
     mixed_sent = mixed.reshape(local_blocks, peer_count, right_local, row_count)
-    mixed_got = lax.all_to_all(mixed_sent, "blk", split_axis=1, concat_axis=0, tiled=True)
+    mixed_got = perform_layers_all(mixed_sent)
     permuted = mixed_got.reshape(order_right, right_local, row_count)
     upstream = cotangent.reshape(row_count, right_local, order_right)
     right_full = lax.all_gather(right_factor, "bin", axis=1, tiled=True)

time: 176 us -> 168 us (0.955)
  waiting for transfers between devices: 117 us -> 58.3 us
  starting transfers between devices: 10.2 us -> 53 us
  local copies, waits for them, and re-layouts: 11.3 us -> 20.5 us
    ppermute x0 -> x7, starting transfers between devices: none -> 45.5 us  [step_on_series_all(): ppermute(top, axis_name=axis_id, perm=list(map(lambda pp: (pp, (pp + k) %...]
    all_to_all x1, waiting for transfers between devices: 43.4 us -> 0.01 us  [on_device(): lax.all_to_all(back_sent, 'blk', split_axis=1, concat_axis=0, tiled=True)]
    all_to_all x1 -> x0, waiting for transfers between devices: 40.7 us -> none  [on_device(): lax.all_to_all(mixed_sent, 'blk', split_axis=1, concat_axis=0, tiled=True)]
    ppermute x0 -> x7, waiting for transfers between devices: none -> 29.2 us  [step_on_series_all(): ppermute(top, axis_name=axis_id, perm=list(map(lambda pp: (pp, (pp + k) %...]
    all_gather x1, waiting for transfers between devices: 18 us -> 2.36 us  [on_device(): left_full = lax.all_gather(left_factor, 'bin', axis=1, tiled=True)]
    reduce_scatter x1, waiting for transfers between devices: 0.02 us -> 7.77 us  [on_device(): lax.psum_scatter(right_term, 'bin', scatter_dimension=1, tiled=True)]
    dynamic_update_slice x0 -> x8, local copies, waits for them, and re-layouts: none -> 7.08 us  [step_on_series_all(): lax.dynamic_update_slice_in_dim(all_rows, arr_out, v_next, axis=0)]
    all_to_all x1 -> x0, starting transfers between devices: 5.77 us -> none  [on_device(): lax.all_to_all(mixed_sent, 'blk', split_axis=1, concat_axis=0, tiled=True)]
  transfers between devices with their start and end apart: 5 -> 11, of which waited for: 4 -> 6; matrix products, arithmetic and copies ran while one was open for 11% -> 22% of each run, Pallas kernels for 0% -> 0%
where the time goes in v1:
time: 168 us
  waiting for transfers between devices  58.3 us (35%)
  starting transfers between devices  53 us (32%)
  local copies, waits for them, and re-layouts  20.5 us (12%)
  between operations  13.9 us (8%)
  matrix products  13.5 us (8%)
  other arithmetic  5.95 us (4%)
  blocking collectives  2.64 us (2%)
    ppermute x7, starting transfers between devices, step_on_series_all(): ppermute(top, axis_name=axis_id, perm=list(map(lambda pp: (pp, (pp + k) %...  45.5 us
    ppermute x7, waiting for transfers between devices, step_on_series_all(): ppermute(top, axis_name=axis_id, perm=list(map(lambda pp: (pp, (pp + k) %...  29.2 us
    reduce_scatter x1, waiting for transfers between devices, on_device(): lax.psum_scatter(left_term, 'bin', scatter_dimension=1, tiled=True)  18.3 us
    reduce_scatter x1, waiting for transfers between devices, on_device(): lax.psum_scatter(right_term, 'bin', scatter_dimension=1, tiled=True)  7.77 us
    all_to_all x1, starting transfers between devices, on_device(): lax.all_to_all(back_sent, 'blk', split_axis=1, concat_axis=0, tiled=True)  7.3 us
    dynamic_update_slice x8, local copies, waits for them, and re-layouts, step_on_series_all(): lax.dynamic_update_slice_in_dim(all_rows, arr_out, v_next, axis=0)  7.08 us
    dot_general x1, matrix products, on_device(): jnp.einsum('rki,kij->kjr', inputs, left_full, preferred_element_type=jnp....  5.44 us
    dot_general x1, matrix products, on_device(): jnp.einsum('rki,jkr->kij', inputs, returned, preferred_element_type=jnp.f...  4.65 us
  transfers between devices with their start and end apart: 11, of which 6 were waited for; matrix products, arithmetic and copies ran while one was open for 22% of the time, Pallas kernels for 0%

profile of v1, /device:TPU:0, one launch (start us, length us, event | category | flops | bytes accessed | tf_op | source)
XLA Modules:
  0.0 167.9 jit_solution(15973174507466853445)
XLA Ops:
  7.2 0.0 all-gather.2.cloned.1.call-start
  7.2 0.7 all-gather.2.cloned.1.call-update
  7.9 0.0 copy-start.1
  7.9 3.3 %copy.26 = bf16[256,4096]{0,1:T(8,128)(2,1)S(1)} copy(bf16[256,4096]{1,0:T(8,128)(2,1)} %param.6) | data formatting | bytes 4194304 | tf_op args[1]
  11.3 2.6 %all_gather.6 = bf16[64,64,64]{2,1,0:T(8,128)(2,1)S(1)} all-gather(bf16[64,32,64]{2,1,0:T(8,128)(2,1)S(1)} %copy-done.1), channel_id=1, replica_groups=mesh['grp'=2,'blk'=8,'bin'=2] {'bin'}, dimensions={1}, use_global_device_ids=true | all-gather | bytes 786432 | tf_op jit(solution)/shard_map/all_gather | solution.py:61
  13.9 0.7 convert_bitcast_fusion.1
  14.6 1.5 copy.27
  16.1 7.3 %all-to-all-start = ((bf16[64,8,8,256]{3,2,0,1:T(8,128)(2,1)}), bf16[64,8,8,256]{3,2,0,1:T(8,128)(2,1)}, u32[]{:S(2)}, u32[]{:S(2)}) async-start(bf16[64,8,8,256]{3,2,0,1:T(8,128)(2,1)} %copy.27), calls=%async_computation | async-start | bytes 4194304 | tf_op jit(solution)/shard_map/all_to_all | solution.py:66
  23.4 0.0 reduce-scatter.5.cloned.1.call-start
  23.5 0.1 fusion.5
  23.6 2.4 %all-gather.2.cloned.1.call-done = bf16[8,512,512]{2,1,0:T(8,128)(2,1)} async-done(((bf16[8,256,512]{2,1,0:T(8,128)(2,1)}), bf16[8,512,512]{2,1,0:T(8,128)(2,1)}) %all-gather.2.cloned.1.call-update) | async-done | bytes 4194320 | tf_op jit(solution)/shard_map/all_gather | solution.py:53
  25.9 5.4 %convert_bitcast_fusion = bf16[8,512,256]{1,2,0:T(8,128)(2,1)} fusion(bf16[8,512,512]{2,1,0:T(8,128)(2,1)} %all-gather.2.cloned.1.call-done, bf16[32,8,8,512]{3,2,1,0:T(8,128)(2,1)} %bitcast.43, bf16[8,512]{1,0:T(8,128)(2,1)S(1)} %fusion.5), kind=kOutput, calls=%fused_computation.3 | convolution fusion | flops 1075838976 | bytes 8396800 | tf_op jit(solution)/shard_map/rki,kij->kjr/dot_general | solution.py:54
  31.4 3.9 %copy.30 = bf16[8,512,256]{2,1,0:T(8,128)(2,1)} copy(bf16[8,512,256]{1,2,0:T(8,128)(2,1)} %convert_bitcast_fusion) | data formatting | bytes 4194304 | tf_op jit(solution)/shard_map/convert_element_type | solution.py:56
  35.3 2.5 %dynamic-slice_bitcast_fusion = (bf16[1,8,1,64,256]{4,3,0,1,2:T(8,128)(2,1)S(1)}, bf16[1,8,1,64,256]{4,3,0,1,2:T(8,128)(2,1)S(1)}, bf16[1,8,1,64,256]{4,3,0,1,2:...) fusion(bf16[8,8,1,64,256]{4,3,1,0,2:T(8,128)(2,1)} %bitcast.39,, ...), kind=kLoop, calls=%fused_computation.8 | loop fusion | bytes 3670044 | tf_op jit(solution)/shard_map/jit(dynamic_index_in_dim)/dynamic_slice | solution.py:30
  37.8 1.7 %collective-permute-start = (bf16[1,8,1,64,256]{4,3,0,1,2:T(8,128)(2,1)}, bf16[1,8,1,64,256]{4,3,0,1,2:T(8,128)(2,1)S(1)}, u32[]{:S(2)}, u32[]{:S(2)}) collective-permute-start(bf16[1,8,1,64,256]{4,3,0,1,2:T(8,128)(2,1)} %get-tuple-element.8), channel_id=1, source_target_pairs={{0,2},{2,4},{4,6},{6,8},{8,10},{10,12},{12,14},{14,0},{1,3},{3,5},... | collective-permute-start | bytes 786440 | tf_op jit(solution)/shard_map/ppermute | solution.py:31
  39.6 1.5 collective-permute-start.1
  41.0 2.4 %collective-permute-start.2 = (bf16[1,8,1,64,256]{4,3,0,1,2:T(8,128)(2,1)}, bf16[1,8,1,64,256]{4,3,0,1,2:T(8,128)(2,1)S(1)}, u32[]{:S(2)}, u32[]{:S(2)}) collective-permute-start(bf16[1,8,1,64,256]{4,3,0,1,2:T(8,128)(2,1)} %get-tuple-element.6), channel_id=1, source_target_pairs={{0,6},{2,8},{4,10},{6,12},{8,14},{10,0},{12,2},{14,4},{1,7},{3,9},... | collective-permute-start | bytes 786440 | tf_op jit(solution)/shard_map/ppermute | solution.py:31
  43.4 2.3 %collective-permute-start.6 = (bf16[1,8,1,64,256]{4,3,0,1,2:T(8,128)(2,1)S(1)}, bf16[1,8,1,64,256]{4,3,0,1,2:T(8,128)(2,1)S(1)}, u32[]{:S(2)}, u32[]{:S(2)}) collective-permute-start(bf16[1,8,1,64,256]{4,3,0,1,2:T(8,128)(2,1)S(1)} %get-tuple-element.2), channel_id=1, source_target_pairs={{0,14},{2,0},{4,2},{6,4},{8,6},{10,8},{12,10},{14,12},{1,15},{3,1}... | collective-permute-start | bytes 786440 | tf_op jit(solution)/shard_map/ppermute | solution.py:31
  45.8 0.5 collective-permute-start.5
  46.3 23.0 %collective-permute-done = bf16[1,8,1,64,256]{4,3,0,1,2:T(8,128)(2,1)S(1)} collective-permute-done((bf16[1,8,1,64,256]{4,3,0,1,2:T(8,128)(2,1)}, bf16[1,8,1,64,256]{4,3,0,1,2:T(8,128)(2,1)S(1)}, u32[]{:S(2)}, u32[]{:S(2)}) %collective-permute-start) | collective-permute-done | bytes 262176 | tf_op jit(solution)/shard_map/ppermute | solution.py:31
  69.3 32.2 %collective-permute-start.3 = (bf16[1,8,1,64,256]{4,3,0,1,2:T(8,128)(2,1)}, bf16[1,8,1,64,256]{4,3,0,1,2:T(8,128)(2,1)S(1)}, u32[]{:S(2)}, u32[]{:S(2)}) collective-permute-start(bf16[1,8,1,64,256]{4,3,0,1,2:T(8,128)(2,1)} %get-tuple-element.5), channel_id=1, source_target_pairs={{0,8},{2,10},{4,12},{6,14},{8,0},{10,2},{12,4},{14,6},{1,9},{3,11}... | collective-permute-start | bytes 786440 | tf_op jit(solution)/shard_map/ppermute | solution.py:31
  101.5 0.8 constant_dynamic-update-slice_fusion.6
  102.3 0.0 collective-permute-done.1
  102.3 4.8 %collective-permute-start.4 = (bf16[1,8,1,64,256]{4,3,0,1,2:T(8,128)(2,1)}, bf16[1,8,1,64,256]{4,3,0,1,2:T(8,128)(2,1)S(1)}, u32[]{:S(2)}, u32[]{:S(2)}) collective-permute-start(bf16[1,8,1,64,256]{4,3,0,1,2:T(8,128)(2,1)} %get-tuple-element.4), channel_id=1, source_target_pairs={{0,10},{2,12},{4,14},{6,0},{8,2},{10,4},{12,6},{14,8},{1,11},{3,13... | collective-permute-start | bytes 786440 | tf_op jit(solution)/shard_map/ppermute | solution.py:31
  107.2 0.8 constant_dynamic-update-slice_fusion.5
  107.9 0.0 collective-permute-done.2
  107.9 0.7 constant_dynamic-update-slice_fusion.4
  108.7 5.8 %collective-permute-done.3 = bf16[1,8,1,64,256]{4,3,0,1,2:T(8,128)(2,1)S(1)} collective-permute-done((bf16[1,8,1,64,256]{4,3,0,1,2:T(8,128)(2,1)}, bf16[1,8,1,64,256]{4,3,0,1,2:T(8,128)(2,1)S(1)}, u32[]{:S(2)}, u32[]{:S(2)}) %collective-permute-start.3) | collective-permute-done | bytes 262176 | tf_op jit(solution)/shard_map/ppermute | solution.py:31
  114.5 0.7 constant_dynamic-update-slice_fusion.3
  115.2 0.3 collective-permute-done.4
  115.6 0.7 constant_dynamic-update-slice_fusion.2
  116.3 0.0 collective-permute-done.5
  116.3 0.8 constant_dynamic-update-slice_fusion.1
  117.1 0.0 collective-permute-done.6
  117.1 0.7 constant_dynamic-update-slice_fusion
  117.8 1.8 %copy.31 = bf16[8,8,1,64,256]{4,3,1,0,2:T(8,128)(2,1)S(1)} copy(bf16[8,8,1,64,256]{4,3,0,1,2:T(8,128)(2,1)} %constant_dynamic-update-slice_fusion) | data formatting | bytes 4194304 | tf_op jit(solution)/shard_map/dynamic_update_slice | solution.py:36
  119.6 2.8 %fusion = f32[64,64,64]{2,1,0:T(8,128)} fusion(bf16[256,64,64]{0,2,1:T(8,128)(2,1)S(1)} %bitcast.38, bf16[64,64,256]{2,1,0:T(8,128)(2,1)S(1)} %bitcast.41), kind=kOutput, calls=%fused_computation.1 | convolution fusion | flops 134217728 | bytes 5242880 | tf_op jit(solution)/shard_map/kjr,rjm->jkm/dot_general | solution.py:68
  122.4 0.0 reduce-scatter.5.cloned.1.call-update
  122.4 0.0 reduce-scatter.3.cloned.1.call-start
  122.5 0.0 all-to-all-done
  122.5 0.0 copy-start
  122.5 2.2 %copy.28 = bf16[8,64,1,8,256]{4,1,0,3,2:T(8,128)(2,1)S(1)} copy(bf16[8,64,1,8,256]{4,3,1,0,2:T(8,128)(2,1)} %bitcast.3) | data formatting | bytes 4194304 | tf_op jit(solution)/shard_map/all_to_all | solution.py:66
  124.7 4.6 %fusion.2 = f32[8,512,512]{2,1,0:T(8,128)} fusion(bf16[512,8,256]{2,0,1:T(8,128)(2,1)S(1)} %bitcast.42, bf16[32,8,8,512]{3,2,1,0:T(8,128)(2,1)S(1)} %bitcast.44, bf16[8,512]{1,0:T(8,128)(2,1)S(1)} %fusion.5), kind=kOutput, calls=%fused_computation.5 | convolution fusion | flops 1074790400 | bytes 12591104 | tf_op jit(solution)/shard_map/rki,jkr->kij/dot_general | solution.py:72
  129.4 0.0 reduce-scatter.3.cloned.1.call-update
  129.4 7.8 %reduce-scatter.5.cloned.1.call-done = f32[64,32,64]{2,1,0:T(8,128)} async-done(((f32[64,64,64]{2,1,0:T(8,128)}), f32[64,32,64]{2,1,0:T(8,128)}) %reduce-scatter.5.cloned.1.call-update) | async-done | bytes 524304 | tf_op jit(solution)/shard_map/reduce_scatter | solution.py:69
  137.2 2.1 %convert_element_type.27 = bf16[64,32,64]{2,1,0:T(8,128)(2,1)} convert(f32[64,32,64]{2,1,0:T(8,128)} %reduce-scatter.5.cloned.1.call-done) | non-fusion elementwise | flops 131072 | bytes 786432 | tf_op jit(solution)/shard_map/convert_element_type | solution.py:69
  139.3 18.3 %reduce-scatter.3.cloned.1.call-done = f32[8,256,512]{2,1,0:T(8,128)} async-done(((f32[8,512,512]{2,1,0:T(8,128)}), f32[8,256,512]{2,1,0:T(8,128)}) %reduce-scatter.3.cloned.1.call-update) | async-done | bytes 4194320 | tf_op jit(solution)/shard_map/reduce_scatter | solution.py:73
  157.6 3.8 %convert_element_type.24 = bf16[8,256,512]{2,1,0:T(8,128)(2,1)} convert(f32[8,256,512]{2,1,0:T(8,128)} %reduce-scatter.3.cloned.1.call-done) | non-fusion elementwise | flops 1048576 | bytes 6291456 | tf_op jit(solution)/shard_map/convert_element_type | solution.py:73
  (4 shorter events, 0.0 us)
Async XLA Ops:
  7.2 18.8 %all-gather.2.cloned.1.call-start = ((), (), s32[]{:S(2)}) async-start(), calls=%async_computation.4 | async-start | bytes 6291456 | tf_op jit(solution)/shard_map/all_gather | solution.py:53
  7.9 3.4 %copy-start.1 = (bf16[64,32,64]{2,1,0:T(8,128)(2,1)S(1)}, bf16[64,32,64]{2,1,0:T(8,128)(2,1)}, u32[]{:S(2)}) copy-start(bf16[64,32,64]{2,1,0:T(8,128)(2,1)} %param.8) | copy-start | bytes 786436
  16.1 7.5 %copy-start.2 = (s32[8]{0:T(128)S(1)}, s32[8]{0:T(128)}, u32[]{:S(2)}) copy-start(s32[8]{0:T(128)} %param.9) | copy-start | bytes 100
  16.1 106.4 %all-to-all-start = ((bf16[64,8,8,256]{3,2,0,1:T(8,128)(2,1)}), bf16[64,8,8,256]{3,2,0,1:T(8,128)(2,1)}, u32[]{:S(2)}, u32[]{:S(2)}) async-start(bf16[64,8,8,256]{3,2,0,1:T(8,128)(2,1)} %copy.27), calls=%async_computation | async-start | bytes 4194304 | tf_op jit(solution)/shard_map/all_to_all | solution.py:66
  23.4 113.8 %reduce-scatter.5.cloned.1.call-start = ((), (), s32[]{:S(2)}) async-start(), calls=%async_computation.5 | async-start | bytes 3145728 | tf_op jit(solution)/shard_map/reduce_scatter | solution.py:69
  37.8 31.5 %collective-permute-start = (bf16[1,8,1,64,256]{4,3,0,1,2:T(8,128)(2,1)}, bf16[1,8,1,64,256]{4,3,0,1,2:T(8,128)(2,1)S(1)}, u32[]{:S(2)}, u32[]{:S(2)}) collective-permute-start(bf16[1,8,1,64,256]{4,3,0,1,2:T(8,128)(2,1)} %get-tuple-element.8), channel_id=1, source_target_pairs={{0,2},{2,4},{4,6},{6,8},{8,10},{10,12},{12,14},{14,0},{1,3},{3,5},... | collective-permute-start | bytes 786440 | tf_op jit(solution)/shard_map/ppermute | solution.py:31
  39.6 62.8 %collective-permute-start.1 = (bf16[1,8,1,64,256]{4,3,0,1,2:T(8,128)(2,1)}, bf16[1,8,1,64,256]{4,3,0,1,2:T(8,128)(2,1)S(1)}, u32[]{:S(2)}, u32[]{:S(2)}) collective-permute-start(bf16[1,8,1,64,256]{4,3,0,1,2:T(8,128)(2,1)} %get-tuple-element.7), channel_id=1, source_target_pairs={{0,4},{2,6},{4,8},{6,10},{8,12},{10,14},{12,0},{14,2},{1,5},{3,7},... | collective-permute-start | bytes 786440 | tf_op jit(solution)/shard_map/ppermute | solution.py:31
  41.0 66.9 %collective-permute-start.2 = (bf16[1,8,1,64,256]{4,3,0,1,2:T(8,128)(2,1)}, bf16[1,8,1,64,256]{4,3,0,1,2:T(8,128)(2,1)S(1)}, u32[]{:S(2)}, u32[]{:S(2)}) collective-permute-start(bf16[1,8,1,64,256]{4,3,0,1,2:T(8,128)(2,1)} %get-tuple-element.6), channel_id=1, source_target_pairs={{0,6},{2,8},{4,10},{6,12},{8,14},{10,0},{12,2},{14,4},{1,7},{3,9},... | collective-permute-start | bytes 786440 | tf_op jit(solution)/shard_map/ppermute | solution.py:31
  43.4 73.6 %collective-permute-start.6 = (bf16[1,8,1,64,256]{4,3,0,1,2:T(8,128)(2,1)S(1)}, bf16[1,8,1,64,256]{4,3,0,1,2:T(8,128)(2,1)S(1)}, u32[]{:S(2)}, u32[]{:S(2)}) collective-permute-start(bf16[1,8,1,64,256]{4,3,0,1,2:T(8,128)(2,1)S(1)} %get-tuple-element.2), channel_id=1, source_target_pairs={{0,14},{2,0},{4,2},{6,4},{8,6},{10,8},{12,10},{14,12},{1,15},{3,1}... | collective-permute-start | bytes 786440 | tf_op jit(solution)/shard_map/ppermute | solution.py:31
  45.8 70.5 %collective-permute-start.5 = (bf16[1,8,1,64,256]{4,3,0,1,2:T(8,128)(2,1)S(1)}, bf16[1,8,1,64,256]{4,3,0,1,2:T(8,128)(2,1)S(1)}, u32[]{:S(2)}, u32[]{:S(2)}) collective-permute-start(bf16[1,8,1,64,256]{4,3,0,1,2:T(8,128)(2,1)S(1)} %get-tuple-element.3), channel_id=1, source_target_pairs={{0,12},{2,14},{4,0},{6,2},{8,4},{10,6},{12,8},{14,10},{1,13},{3,15... | collective-permute-start | bytes 786440 | tf_op jit(solution)/shard_map/ppermute | solution.py:31
  69.3 45.2 %collective-permute-start.3 = (bf16[1,8,1,64,256]{4,3,0,1,2:T(8,128)(2,1)}, bf16[1,8,1,64,256]{4,3,0,1,2:T(8,128)(2,1)S(1)}, u32[]{:S(2)}, u32[]{:S(2)}) collective-permute-start(bf16[1,8,1,64,256]{4,3,0,1,2:T(8,128)(2,1)} %get-tuple-element.5), channel_id=1, source_target_pairs={{0,8},{2,10},{4,12},{6,14},{8,0},{10,2},{12,4},{14,6},{1,9},{3,11}... | collective-permute-start | bytes 786440 | tf_op jit(solution)/shard_map/ppermute | solution.py:31
  102.3 13.2 %collective-permute-start.4 = (bf16[1,8,1,64,256]{4,3,0,1,2:T(8,128)(2,1)}, bf16[1,8,1,64,256]{4,3,0,1,2:T(8,128)(2,1)S(1)}, u32[]{:S(2)}, u32[]{:S(2)}) collective-permute-start(bf16[1,8,1,64,256]{4,3,0,1,2:T(8,128)(2,1)} %get-tuple-element.4), channel_id=1, source_target_pairs={{0,10},{2,12},{4,14},{6,0},{8,2},{10,4},{12,6},{14,8},{1,11},{3,13... | collective-permute-start | bytes 786440 | tf_op jit(solution)/shard_map/ppermute | solution.py:31
  122.4 35.2 %reduce-scatter.3.cloned.1.call-start = ((), (), s32[]{:S(2)}) async-start(), calls=%async_computation.3 | async-start | bytes 12582912 | tf_op jit(solution)/shard_map/reduce_scatter | solution.py:73
  122.5 2.2 %copy-start = (bf16[256,4096]{1,0:T(8,128)(2,1)S(1)}, bf16[256,4096]{1,0:T(8,128)(2,1)}, u32[]{:S(2)}) copy-start(bf16[256,4096]{1,0:T(8,128)(2,1)} %param.5) | copy-start | bytes 6291460
Sparse Core Ops, SparseCore 0:
  9.5 16.3 all-gather.1
  122.5 14.5 reduce-scatter.4
  139.6 17.9 reduce-scatter.2
